TPU v7x, 128 devices: a whole 4x4x4 slice. The times are simulated.
128 devices in a mesh: row: 8 (over z, core), col: 8 (over y_hi, x), dp: 2 (over y_lo).
Axes of the slice: x: 4, y: 4 (y_hi: 2, y_lo: 2; y = y_hi * 2 + y_lo), z: 4, core: 2. Of those that a mesh axis runs over, the one named last changes fastest.
Arguments:
- tokens: bfloat16 [2048, 4096], P(('col', 'dp'), 'row'), may hold values from -6 to 6
- timesteps: int32 [8], replicated, may hold values from 0 to 999
- ada_weight: bfloat16 [3, 4096, 4096], P(None, 'col', 'row'), may hold values from -0.09375 to 0.09375
- up_weight: bfloat16 [4096, 16384], P('row', 'col'), may hold values from -0.90625 to 0.90625
- down_weight: bfloat16 [16384, 4096], P('col', 'row'), may hold values from -0.046875 to 0.046875
- cotangent: bfloat16 [2048, 4096], P(('col', 'dp'), 'row'), may hold values from -6 to 6
Outputs:
- grad_tokens: bfloat16 [2048, 4096], P(('col', 'dp'), 'row')
- grad_ada: float32 [3, 4096, 4096], P(None, 'col', 'row')
- grad_up: float32 [4096, 16384], P('row', ('col', 'dp'))
- grad_down: float32 [16384, 4096], P(('col', 'dp'), 'row')
All inputs are finite; a program needn't handle non-finite values.
Results may differ from a plain program's by a relative error of at most 0.04.
Values may be sent and summed in bfloat16 or wider, within the bound.
No kernel may reach another device: no remote copies, remote signals or barrier semaphores. Data moves between devices by JAX's collectives and lax.ppermute only.
A program may use at most 128 MiB of HBM per device.

v0:
```python
import math
import jax
import jax.numpy as jnp
from jax import lax
from jax.sharding import PartitionSpec as P

tanh_scale = math.sqrt(2.0 / math.pi)


def gelu_tanh(h):
    return 0.5 * h * (1.0 + jnp.tanh(tanh_scale * (h + 0.044715 * h * h * h)))


def gelu_slope(h):
    inner = jnp.tanh(tanh_scale * (h + 0.044715 * h * h * h))
    return 0.5 * (1.0 + inner) + 0.5 * h * (1.0 - inner * inner) * tanh_scale * (
        1.0 + 3.0 * 0.044715 * h * h
    )


def time_features(timesteps, width):
    half = width // 2
    freqs = jnp.exp(-math.log(10000.0) * jnp.arange(half, dtype=jnp.float32) / half)
    angles = timesteps.astype(jnp.float32)[:, None] * freqs[None, :]
    embed = jnp.concatenate([jnp.cos(angles), jnp.sin(angles)], axis=1)
    return jax.nn.silu(embed).astype(jnp.bfloat16)


def body(tokens, timesteps, ada_weight, up_weight, down_weight, cotangent):
    rows_count = lax.axis_size("row")
    cols_count = lax.axis_size("col")
    col_index = lax.axis_index("col")
    tok_rows, width = tokens.shape
    full_width = width * rows_count
    in_width = ada_weight.shape[1]
    cond = time_features(timesteps, full_width)
    cond_part = lax.dynamic_slice_in_dim(cond, col_index * in_width, in_width, 1)
    mod_terms = jnp.einsum("vi,kio->vko", cond_part, ada_weight, preferred_element_type=jnp.float32)
    mod = lax.psum(mod_terms.astype(jnp.bfloat16), "col").astype(jnp.float32)
    own_mod = lax.dynamic_index_in_dim(mod, col_index, 0, keepdims=False)
    shift = own_mod[0]
    scale = own_mod[1]
    gate = own_mod[2]
    x = tokens.astype(jnp.float32)
    total, squares = lax.psum((jnp.sum(x, axis=1), jnp.sum(x * x, axis=1)), "row")
    mean = total / full_width
    var = squares / full_width - mean * mean
    rstd = lax.rsqrt(var + 1e-06)
    normed = (x - mean[:, None]) * rstd[:, None]
    modulated = (normed * (1.0 + scale) + shift).astype(jnp.bfloat16)
    mod_full = lax.all_gather(modulated, "col", axis=0, tiled=True)
    picked = mod_full
    hidden_own = lax.psum_scatter(
        jnp.dot(picked, up_weight, preferred_element_type=jnp.float32).astype(jnp.bfloat16),
        "row",
        scatter_dimension=0,
        tiled=True,
    ).astype(jnp.float32)
    act_own = gelu_tanh(hidden_own).astype(jnp.bfloat16)
    act_full = lax.all_gather(act_own, "row", axis=0, tiled=True)
    picked = act_full
    branch = lax.psum_scatter(
        jnp.dot(picked, down_weight, preferred_element_type=jnp.float32).astype(jnp.bfloat16),
        "col",
        scatter_dimension=0,
        tiled=True,
    ).astype(jnp.float32)
    cot = cotangent.astype(jnp.float32)
    grad_branch = (cot * gate).astype(jnp.bfloat16)
    grad_gate = jnp.sum(cot * branch, axis=0)
    branch_full = lax.all_gather(grad_branch, "col", axis=0, tiled=True)
    mod_full = lax.all_gather(modulated, "col", axis=0, tiled=True)
    act_full = lax.all_gather(act_own, "row", axis=0, tiled=True)
    down_part = lax.dot_general(
        act_full, branch_full, (((0,), (0,)), ((), ())), preferred_element_type=jnp.float32
    )
    picked = branch_full
    grad_act = lax.psum_scatter(
        lax.dot_general(
            picked, down_weight, (((1,), (1,)), ((), ())), preferred_element_type=jnp.float32
        ).astype(jnp.bfloat16),
        "row",
        scatter_dimension=0,
        tiled=True,
    ).astype(jnp.float32)
    grad_hidden = (grad_act * gelu_slope(hidden_own)).astype(jnp.bfloat16)
    grad_full = lax.all_gather(grad_hidden, "row", axis=0, tiled=True)
    up_part = lax.dot_general(
        mod_full, grad_full, (((0,), (0,)), ((), ())), preferred_element_type=jnp.float32
    )
    picked = grad_full
    grad_mod_in = lax.psum_scatter(
        lax.dot_general(
            picked, up_weight, (((1,), (1,)), ((), ())), preferred_element_type=jnp.float32
        ).astype(jnp.bfloat16),
        "col",
        scatter_dimension=0,
        tiled=True,
    ).astype(jnp.float32)
    grad_up, grad_down = (
        lax.psum_scatter(
            up_part.astype(jnp.bfloat16), "dp", scatter_dimension=1, tiled=True
        ).astype(jnp.float32),
        lax.psum_scatter(
            down_part.astype(jnp.bfloat16), "dp", scatter_dimension=0, tiled=True
        ).astype(jnp.float32),
    )
    grad_norm = grad_mod_in * (1.0 + scale)
    first, second = lax.psum(
        (jnp.sum(grad_norm, axis=1), jnp.sum(grad_norm * normed, axis=1)), "row"
    )
    first = first / full_width
    second = second / full_width
    grad_tokens = cot + rstd[:, None] * (grad_norm - first[:, None] - normed * second[:, None])
    own_grad = jnp.stack(
        [jnp.sum(grad_mod_in, axis=0), jnp.sum(grad_mod_in * normed, axis=0), grad_gate], axis=0
    )
    selector = (jnp.arange(cols_count, dtype=jnp.int32) == col_index).astype(jnp.float32)
    placed = selector[:, None, None] * own_grad[None, :, :]
    grad_mod = lax.psum(placed.astype(jnp.bfloat16), ("col", "dp")).astype(jnp.float32)
    grad_ada = jnp.einsum(
        "vi,vko->kio", cond_part.astype(jnp.float32), grad_mod, precision=lax.Precision.HIGHEST
    )
    return (grad_tokens.astype(jnp.bfloat16), grad_ada, grad_up, grad_down)


def solution(mesh):
    return jax.shard_map(
        body,
        mesh=mesh,
        in_specs=(
            P(("col", "dp"), "row"),
            P(),
            P(None, "col", "row"),
            P("row", "col"),
            P("col", "row"),
            P(("col", "dp"), "row"),
        ),
        out_specs=(
            P(("col", "dp"), "row"),
            P(None, "col", "row"),
            P("row", ("col", "dp")),
            P(("col", "dp"), "row"),
        ),
        check_vma=False,
    )
```

profile of v0, /device:TPU:0, one launch (start us, length us, event | category | flops | bytes accessed | tf_op | source)
XLA Modules:
  0.0 550.7 jit_solution(17362788977848606605)
XLA Ops:
  7.2 0.0 all-gather.7.cloned.1.call-start
  7.3 0.8 convert_element_type.83
  8.1 1.0 fusion.20
  9.1 0.3 multiply_cosine_fusion
  9.4 1.7 convolution_convert_fusion.6
  11.1 42.0 %psum.44 = bf16[8,3,512]{2,0,1:T(8,128)(2,1)S(1)} all-reduce(bf16[8,3,512]{2,0,1:T(8,128)(2,1)S(1)} %convolution_convert_fusion.6), channel_id=1, replica_groups=mesh['row'=8,'col'=8,'dp'=2] {'col'}, use_global_device_ids=true, to_apply=%region_4.5 | all-reduce | flops 12288 | bytes 49152 | tf_op jit(solution)/shard_map/psum | solution.py:39
  53.2 13.1 %all-reduce.1 = (f32[128]{0:T(128)S(1)}, f32[128]{0:T(128)S(1)}) all-reduce(f32[128]{0:T(128)S(1)} %get-tuple-element.13, f32[128]{0:T(128)S(1)} %get-tuple-element.12), channel_id=1, replica_groups=mesh['row'=8,'col'=8,'dp'=2] {'row'}, use_global_device_ids=true, to_apply=%region_3.4 | all-reduce | flops 256 | bytes 2048 | tf_op jit(solution)/shard_map/psum | solution.py:45
  66.3 0.8 fusion.25
  67.1 0.0 all-gather.7.cloned.1.call-update
  67.1 0.0 all-gather.5.cloned.1.call-start
  67.2 0.7 fusion.17
  67.9 0.0 all-gather.5.cloned.1.call-update
  67.9 0.0 reduce-scatter.9.cloned.1.call-start
  68.0 41.2 %all-gather.7.cloned.1.call-done = bf16[1024,512]{1,0:T(8,128)(2,1)} async-done(((bf16[128,512]{1,0:T(8,128)(2,1)}), bf16[1024,512]{1,0:T(8,128)(2,1)}) %all-gather.7.cloned.1.call-update) | async-done | bytes 1048592 | tf_op jit(solution)/shard_map/all_gather | solution.py:51
  109.1 5.5 convolution_convert_fusion
  114.7 0.0 reduce-scatter.7.cloned.1.call-start
  114.7 43.4 %all-gather.5.cloned.1.call-done = bf16[1024,512]{1,0:T(8,128)(2,1)} async-done(((bf16[128,512]{1,0:T(8,128)(2,1)}), bf16[1024,512]{1,0:T(8,128)(2,1)}) %all-gather.5.cloned.1.call-update) | async-done | bytes 1048592 | tf_op jit(solution)/shard_map/all_gather | solution.py:71
  158.1 6.3 %convolution_convert_fusion.1 = bf16[1024,2048]{1,0:T(8,128)(2,1)} fusion(bf16[1024,512]{1,0:T(8,128)(2,1)} %all-gather.5.cloned.1.call-done, bf16[2048,512]{1,0:T(8,128)(2,1)} %param.10), kind=kOutput, calls=%fused_computation.1 | convolution fusion | flops 2149580800 | bytes 7340032 | tf_op jit(solution)/shard_map/dot_general | solution.py:79
  164.4 0.0 reduce-scatter.7.cloned.1.call-update
  164.4 0.0 all-gather.9.cloned.1.call-start
  164.5 33.3 %reduce-scatter.9.cloned.1.call-done = bf16[128,2048]{1,0:T(8,128)(2,1)} async-done(((bf16[1024,2048]{1,0:T(8,128)(2,1)}), bf16[128,2048]{1,0:T(8,128)(2,1)}) %reduce-scatter.9.cloned.1.call-update) | async-done | bytes 524304 | tf_op jit(solution)/shard_map/reduce_scatter | solution.py:53
  197.7 39.2 %reduce-scatter.7.cloned.1.call-done = bf16[128,2048]{1,0:T(8,128)(2,1)} async-done(((bf16[1024,2048]{1,0:T(8,128)(2,1)}), bf16[128,2048]{1,0:T(8,128)(2,1)}) %reduce-scatter.7.cloned.1.call-update) | async-done | bytes 524304 | tf_op jit(solution)/shard_map/reduce_scatter | solution.py:78
  237.0 2.9 fusion.7
  239.9 0.0 all-gather.9.cloned.1.call-update
  240.0 0.0 all-gather.11.cloned.1.call-start
  240.0 0.5 all-gather.11.cloned.1.call-update
  240.5 0.0 reduce-scatter.11.cloned.1.call-start
  240.6 30.5 %all-gather.9.cloned.1.call-done = bf16[1024,2048]{1,0:T(8,128)(2,1)} async-done(((bf16[128,2048]{1,0:T(8,128)(2,1)}), bf16[1024,2048]{1,0:T(8,128)(2,1)}) %all-gather.9.cloned.1.call-update) | async-done | bytes 4194320 | tf_op jit(solution)/shard_map/all_gather | solution.py:87
  271.1 5.5 %convolution_convert_fusion.5 = bf16[1024,512]{1,0:T(8,128)(2,1)} fusion(bf16[1024,2048]{1,0:T(8,128)(2,1)} %all-gather.9.cloned.1.call-done, bf16[512,2048]{1,0:T(8,128)(2,1)S(1)} %copy-done), kind=kOutput, calls=%fused_computation.13 | convolution fusion | flops 2148007936 | bytes 7340032 | tf_op jit(solution)/shard_map/dot_general | solution.py:93
  276.7 0.0 reduce-scatter.13.cloned.1.call-start
  276.7 28.6 %all-gather.11.cloned.1.call-done = bf16[1024,2048]{1,0:T(8,128)(2,1)} async-done(((bf16[128,2048]{1,0:T(8,128)(2,1)}), bf16[1024,2048]{1,0:T(8,128)(2,1)}) %all-gather.11.cloned.1.call-update) | async-done | bytes 4194320 | tf_op jit(solution)/shard_map/all_gather | solution.py:60
  305.4 6.2 %convolution_convert_fusion.4 = bf16[1024,512]{1,0:T(8,128)(2,1)} fusion(bf16[1024,2048]{1,0:T(8,128)(2,1)} %all-gather.11.cloned.1.call-done, bf16[2048,512]{1,0:T(8,128)(2,1)} %param.10), kind=kOutput, calls=%fused_computation.12 | convolution fusion | flops 2148007936 | bytes 7340032 | tf_op jit(solution)/shard_map/dot_general | solution.py:63
  311.6 0.0 reduce-scatter.15.cloned.1.call-start
  311.6 5.9 %convolution_convert_fusion.3 = bf16[512,2048]{1,0:T(8,128)(2,1)} fusion(bf16[1024,512]{1,0:T(8,128)(2,1)S(1)} %copy-done.3, bf16[1024,2048]{1,0:T(8,128)(2,1)} %all-gather.9.cloned.1.call-done), kind=kOutput, calls=%fused_computation.3 | convolution fusion | flops 2148532224 | bytes 7340032 | tf_op jit(solution)/shard_map/dot_general | solution.py:88
  317.6 0.2 reduce-scatter.17.cloned.1.call-start
  317.8 1.0 copy-done.4
  318.8 5.9 %convolution_convert_fusion.2 = bf16[2048,512]{1,0:T(8,128)(2,1)} fusion(bf16[1024,2048]{1,0:T(8,128)(2,1)} %all-gather.11.cloned.1.call-done, bf16[1024,512]{1,0:T(8,128)(2,1)S(1)} %copy-done.4), kind=kOutput, calls=%fused_computation.2 | convolution fusion | flops 2148532224 | bytes 7340032 | tf_op jit(solution)/shard_map/dot_general | solution.py:74
  324.7 57.5 %reduce-scatter.11.cloned.1.call-done = bf16[128,512]{1,0:T(8,128)(2,1)} async-done(((bf16[1024,512]{1,0:T(8,128)(2,1)}), bf16[128,512]{1,0:T(8,128)(2,1)}) %reduce-scatter.11.cloned.1.call-update) | async-done | bytes 131088 | tf_op jit(solution)/shard_map/reduce_scatter | solution.py:92
  382.2 1.1 fusion.26
  383.3 12.8 %all-reduce = (f32[128]{0:T(128)S(1)}, f32[128]{0:T(128)S(1)}) all-reduce(f32[128]{0:T(128)S(1)} %get-tuple-element.9, f32[128]{0:T(128)S(1)} %get-tuple-element.10), channel_id=1, replica_groups=mesh['row'=8,'col'=8,'dp'=2] {'row'}, use_global_device_ids=true, to_apply=%region_11.12 | all-reduce | flops 256 | bytes 2048 | tf_op jit(solution)/shard_map/psum | solution.py:109
  396.1 62.1 %reduce-scatter.13.cloned.1.call-done = bf16[128,512]{1,0:T(8,128)(2,1)} async-done(((bf16[1024,512]{1,0:T(8,128)(2,1)}), bf16[128,512]{1,0:T(8,128)(2,1)}) %reduce-scatter.13.cloned.1.call-update) | async-done | bytes 131088 | tf_op jit(solution)/shard_map/reduce_scatter | solution.py:62
  458.1 1.8 fusion.19
  459.9 0.1 multiply_convert_fusion
  460.0 72.4 %psum.47 = bf16[8,3,512]{2,0,1:T(8,128)(2,1)S(1)} all-reduce(bf16[8,3,512]{2,0,1:T(8,128)(2,1)S(1)} %multiply_convert_fusion), channel_id=1, replica_groups=mesh['row'=8,'col'=8,'dp'=2] {'col','dp'}, use_global_device_ids=true, to_apply=%region_16.17 | all-reduce | flops 12288 | bytes 49152 | tf_op jit(solution)/shard_map/psum | solution.py:120
  532.4 2.3 convolution_bitcast_fusion
  534.7 3.5 copy.10
  538.2 2.8 convert_element_type.103
  541.0 2.8 convert_element_type.105
  (23 shorter events, 0.2 us)
Async XLA Ops:
  7.2 102.0 %copy-start = (bf16[512,2048]{1,0:T(8,128)(2,1)S(1)}, bf16[512,2048]{1,0:T(8,128)(2,1)}, u32[]{:S(2)}) copy-start(bf16[512,2048]{1,0:T(8,128)(2,1)} %param.9) | copy-start | bytes 6291460
  7.2 59.2 %copy-start.1 = (bf16[128,512]{1,0:T(8,128)(2,1)S(1)}, bf16[128,512]{1,0:T(8,128)(2,1)}, u32[]{:S(2)}) copy-start(bf16[128,512]{1,0:T(8,128)(2,1)} %param.6) | copy-start | bytes 393220
  7.2 60.0 %copy-start.2 = (bf16[128,512]{1,0:T(8,128)(2,1)S(1)}, bf16[128,512]{1,0:T(8,128)(2,1)}, u32[]{:S(2)}) copy-start(bf16[128,512]{1,0:T(8,128)(2,1)} %param.11) | copy-start | bytes 393220
  7.2 101.9 %all-gather.7.cloned.1.call-start = ((), (), s32[]{:S(2)}) async-start(), calls=%async_computation.8 | async-start | bytes 1179648 | tf_op jit(solution)/shard_map/all_gather | solution.py:51
  67.1 91.0 %all-gather.5.cloned.1.call-start = ((), (), s32[]{:S(2)}) async-start(), calls=%async_computation.6 | async-start | bytes 1179648 | tf_op jit(solution)/shard_map/all_gather | solution.py:71
  67.9 129.8 %reduce-scatter.9.cloned.1.call-start = ((), (), s32[]{:S(2)}) async-start(), calls=%async_computation.9 | async-start | bytes 4718592 | tf_op jit(solution)/shard_map/reduce_scatter | solution.py:53
  114.7 122.3 %reduce-scatter.7.cloned.1.call-start = ((), (), s32[]{:S(2)}) async-start(), calls=%async_computation.7 | async-start | bytes 4718592 | tf_op jit(solution)/shard_map/reduce_scatter | solution.py:78
  164.4 106.7 %all-gather.9.cloned.1.call-start = ((), (), s32[]{:S(2)}) async-start(), calls=%async_computation.10 | async-start | bytes 4718592 | tf_op jit(solution)/shard_map/all_gather | solution.py:87
  240.0 65.4 %all-gather.11.cloned.1.call-start = ((), (), s32[]{:S(2)}) async-start(), calls=%async_computation.12 | async-start | bytes 4718592 | tf_op jit(solution)/shard_map/all_gather | solution.py:60
  240.5 141.7 %reduce-scatter.11.cloned.1.call-start = ((), (), s32[]{:S(2)}) async-start(), calls=%async_computation.11 | async-start | bytes 1179648 | tf_op jit(solution)/shard_map/reduce_scatter | solution.py:92
  276.7 34.9 %copy-start.3 = (bf16[1024,512]{1,0:T(8,128)(2,1)S(1)}, bf16[1024,512]{1,0:T(8,128)(2,1)}, u32[]{:S(2)}) copy-start(bf16[1024,512]{1,0:T(8,128)(2,1)} %all-gather.7.cloned.1.call-done) | copy-start | bytes 3145732
  276.7 181.5 %reduce-scatter.13.cloned.1.call-start = ((), (), s32[]{:S(2)}) async-start(), calls=%async_computation.13 | async-start | bytes 1179648 | tf_op jit(solution)/shard_map/reduce_scatter | solution.py:62
  311.6 226.6 %reduce-scatter.15.cloned.1.call-start = ((), (), s32[]{:S(2)}) async-start(), calls=%async_computation.14 | async-start | bytes 3145728 | tf_op jit(solution)/shard_map/reduce_scatter | solution.py:101
  317.5 1.2 copy-start.4
  317.6 223.4 %reduce-scatter.17.cloned.1.call-start = ((), (), s32[]{:S(2)}) async-start(), calls=%async_computation.15 | async-start | bytes 3145728 | tf_op jit(solution)/shard_map/reduce_scatter | solution.py:104
Sparse Core Ops, SparseCore 0:
  67.3 41.8 all-gather.6
  112.0 46.0 all-gather.4
  160.5 37.1 reduce-scatter.8
  200.0 36.9 reduce-scatter.6
  240.1 31.0 all-gather.8
  273.3 32.0 all-gather.10
  309.6 72.5 reduce-scatter.10
  386.4 71.6 reduce-scatter.12
  461.1 33.8 reduce-scatter.14
  497.1 36.2 reduce-scatter.16
where the time goes:
time: 551 us
  waiting for transfers between devices  336 us (61%)
  blocking collectives  140 us (25%)
  matrix products  39.3 us (7%)
  other arithmetic  15.2 us (3%)
  between operations  14.3 us (3%)
    psum x1, blocking collectives, body(): lax.psum(placed.astype(jnp.bfloat16), ('col', 'dp')).astype(jnp.float32)  72.4 us
    reduce_scatter x1, waiting for transfers between devices, body(): lax.psum_scatter(jnp.dot(picked, down_weight, preferred_element_type=jnp....  62.1 us
    reduce_scatter x1, waiting for transfers between devices, body(): lax.psum_scatter(lax.dot_general(picked, up_weight, (((1,), (1,)), ((), (...  57.5 us
    all_gather x1, waiting for transfers between devices, body(): branch_full = lax.all_gather(grad_branch, 'col', axis=0, tiled=True)  43.4 us
    psum x1, blocking collectives, body(): mod = lax.psum(mod_terms.astype(jnp.bfloat16), 'col').astype(jnp.float32)  42 us
    all_gather x1, waiting for transfers between devices, body(): mod_full = lax.all_gather(modulated, 'col', axis=0, tiled=True)  41.2 us
    reduce_scatter x1, waiting for transfers between devices, body(): lax.psum_scatter(lax.dot_general(picked, down_weight, (((1,), (1,)), ((),...  39.2 us
    reduce_scatter x1, waiting for transfers between devices, body(): lax.psum_scatter(jnp.dot(picked, up_weight, preferred_element_type=jnp.fl...  33.3 us
  transfers between devices with their start and end apart: 10, of which 8 were waited for; matrix products, arithmetic and copies ran while one was open for 9% of the time, Pallas kernels for 0%

commit v1 on v0

--- a/solution.py
+++ b/solution.py
@@ -84,7 +84,15 @@
         tiled=True,
     ).astype(jnp.float32)
     grad_hidden = (grad_act * gelu_slope(hidden_own)).astype(jnp.bfloat16)
-    grad_full = lax.all_gather(grad_hidden, "row", axis=0, tiled=True)
+    grad_full = jnp.concatenate(
+        lax.all_to_all(
+            jnp.stack([grad_hidden for _ in range(lax.axis_size("row"))], 0),
+            axis_name="row",
+            split_axis=0,
+            concat_axis=0,
+        ),
+        axis=0,
+    )
     up_part = lax.dot_general(
         mod_full, grad_full, (((0,), (0,)), ((), ())), preferred_element_type=jnp.float32
     )

time: 551 us -> 592 us (1.074)
  blocking collectives: 140 us -> 209 us
  waiting for transfers between devices: 336 us -> 307 us
    all_to_all x0 -> x1, blocking collectives: none -> 69.1 us  [body(): lax.all_to_all(jnp.stack([grad_hidden for _ in range(lax.axis_size('row')...]
    all_gather x1 -> x0, waiting for transfers between devices: 30.5 us -> none  [body(): grad_full = lax.all_gather(grad_hidden, 'row', axis=0, tiled=True)]
    all_gather x1, waiting for transfers between devices: 28.6 us -> 0.02 us  [body(): act_full = lax.all_gather(act_own, 'row', axis=0, tiled=True)]
    reduce_scatter x1, waiting for transfers between devices: 0.01 us -> 22.4 us  [body(): lax.psum_scatter(up_part.astype(jnp.bfloat16), 'dp', scatter_dimension=1,...]
    reduce_scatter x1, waiting for transfers between devices: 62.1 us -> 75.2 us  [body(): lax.psum_scatter(jnp.dot(picked, down_weight, preferred_element_type=jnp....]
  transfers between devices with their start and end apart: 10 -> 9, of which waited for: 8 -> 7; matrix products, arithmetic and copies ran while one was open for 9% -> 8% of each run, Pallas kernels for 0% -> 0%
where the time goes in v1:
time: 592 us; the launch traced here: 591 us
  waiting for transfers between devices  307 us (52%)
  blocking collectives  209 us (35%)
  matrix products  37.8 us (6%)
  other arithmetic  16.8 us (3%)
  between operations  13.9 us (2%)
  local copies, waits for them, and re-layouts  6.04 us (1%)
    reduce_scatter x1, waiting for transfers between devices, body(): lax.psum_scatter(jnp.dot(picked, down_weight, preferred_element_type=jnp....  75.2 us
    psum x1, blocking collectives, body(): lax.psum(placed.astype(jnp.bfloat16), ('col', 'dp')).astype(jnp.float32)  72.4 us
    all_to_all x1, blocking collectives, body(): lax.all_to_all(jnp.stack([grad_hidden for _ in range(lax.axis_size('row')...  69.1 us
    reduce_scatter x1, waiting for transfers between devices, body(): lax.psum_scatter(lax.dot_general(picked, up_weight, (((1,), (1,)), ((), (...  53 us
    all_gather x1, waiting for transfers between devices, body(): branch_full = lax.all_gather(grad_branch, 'col', axis=0, tiled=True)  43.4 us
    psum x1, blocking collectives, body(): mod = lax.psum(mod_terms.astype(jnp.bfloat16), 'col').astype(jnp.float32)  42 us
    all_gather x1, waiting for transfers between devices, body(): mod_full = lax.all_gather(modulated, 'col', axis=0, tiled=True)  40.3 us
    reduce_scatter x1, waiting for transfers between devices, body(): lax.psum_scatter(lax.dot_general(picked, down_weight, (((1,), (1,)), ((),...  39.2 us
  transfers between devices with their start and end apart: 9, of which 7 were waited for; matrix products, arithmetic and copies ran while one was open for 8% of the time, Pallas kernels for 0%

profile of v1, /device:TPU:0, one launch (start us, length us, event | category | flops | bytes accessed | tf_op | source)
XLA Modules:
  0.0 591.5 jit_solution(8614548376918555776)
XLA Ops:
  7.2 0.0 all-gather.6.cloned.1.call-start
  7.2 0.8 convert_element_type.83
  8.0 1.0 fusion.20
  9.1 0.3 multiply_cosine_fusion
  9.4 1.7 convolution_convert_fusion.6
  11.1 42.0 %psum.44 = bf16[8,3,512]{2,0,1:T(8,128)(2,1)S(1)} all-reduce(bf16[8,3,512]{2,0,1:T(8,128)(2,1)S(1)} %convolution_convert_fusion.6), channel_id=1, replica_groups=mesh['row'=8,'col'=8,'dp'=2] {'col'}, use_global_device_ids=true, to_apply=%region_4.5 | all-reduce | flops 12288 | bytes 49152 | tf_op jit(solution)/shard_map/psum | solution.py:39
  53.2 13.1 %all-reduce.1 = (f32[128]{0:T(128)S(1)}, f32[128]{0:T(128)S(1)}) all-reduce(f32[128]{0:T(128)S(1)} %get-tuple-element.13, f32[128]{0:T(128)S(1)} %get-tuple-element.12), channel_id=1, replica_groups=mesh['row'=8,'col'=8,'dp'=2] {'row'}, use_global_device_ids=true, to_apply=%region_3.4 | all-reduce | flops 256 | bytes 2048 | tf_op jit(solution)/shard_map/psum | solution.py:45
  66.3 1.7 fusion.25
  68.0 0.0 all-gather.6.cloned.1.call-update
  68.0 0.0 all-gather.4.cloned.1.call-start
  68.1 1.6 fusion.17
  69.7 0.0 all-gather.4.cloned.1.call-update
  69.7 0.0 reduce-scatter.9.cloned.1.call-start
  69.7 40.3 %all-gather.6.cloned.1.call-done = bf16[1024,512]{1,0:T(8,128)(2,1)} async-done(((bf16[128,512]{1,0:T(8,128)(2,1)}), bf16[1024,512]{1,0:T(8,128)(2,1)}) %all-gather.6.cloned.1.call-update) | async-done | bytes 1048592 | tf_op jit(solution)/shard_map/all_gather | solution.py:51
  110.0 5.5 convolution_convert_fusion
  115.5 0.0 reduce-scatter.9.cloned.1.call-update
  115.5 0.0 reduce-scatter.7.cloned.1.call-start
  115.6 43.4 %all-gather.4.cloned.1.call-done = bf16[1024,512]{1,0:T(8,128)(2,1)} async-done(((bf16[128,512]{1,0:T(8,128)(2,1)}), bf16[1024,512]{1,0:T(8,128)(2,1)}) %all-gather.4.cloned.1.call-update) | async-done | bytes 1048592 | tf_op jit(solution)/shard_map/all_gather | solution.py:71
  159.0 6.3 %convolution_convert_fusion.1 = bf16[1024,2048]{1,0:T(8,128)(2,1)} fusion(bf16[1024,512]{1,0:T(8,128)(2,1)} %all-gather.4.cloned.1.call-done, bf16[2048,512]{1,0:T(8,128)(2,1)} %param.10), kind=kOutput, calls=%fused_computation.1 | convolution fusion | flops 2149580800 | bytes 7340032 | tf_op jit(solution)/shard_map/dot_general | solution.py:79
  165.3 0.0 all-gather.8.cloned.1.call-start
  165.3 33.3 %reduce-scatter.9.cloned.1.call-done = bf16[128,2048]{1,0:T(8,128)(2,1)} async-done(((bf16[1024,2048]{1,0:T(8,128)(2,1)}), bf16[128,2048]{1,0:T(8,128)(2,1)}) %reduce-scatter.9.cloned.1.call-update) | async-done | bytes 524304 | tf_op jit(solution)/shard_map/reduce_scatter | solution.py:53
  198.6 39.2 %reduce-scatter.7.cloned.1.call-done = bf16[128,2048]{1,0:T(8,128)(2,1)} async-done(((bf16[1024,2048]{1,0:T(8,128)(2,1)}), bf16[128,2048]{1,0:T(8,128)(2,1)}) %reduce-scatter.7.cloned.1.call-update) | async-done | bytes 524304 | tf_op jit(solution)/shard_map/reduce_scatter | solution.py:78
  237.8 2.8 fusion.7
  240.6 0.0 reduce-scatter.11.cloned.1.call-start
  240.7 0.5 stack.10
  241.2 69.1 %all_to_all.5 = bf16[8,128,2048]{2,1,0:T(8,128)(2,1)S(1)} all-to-all(bf16[8,128,2048]{2,1,0:T(8,128)(2,1)S(1)} %stack.10), channel_id=1, replica_groups=mesh['row'=8,'col'=8,'dp'=2] {'row'}, dimensions={0} | all-to-all | bytes 8388608 | tf_op jit(solution)/shard_map/all_to_all | solution.py:88
  310.3 2.0 copy-done.1
  312.2 3.4 convolution_convert_fusion.5
  315.6 0.0 reduce-scatter.11.cloned.1.call-update
  315.6 0.0 reduce-scatter.15.cloned.1.call-start
  315.7 6.2 %convolution_convert_fusion.3 = bf16[512,2048]{1,0:T(8,128)(2,1)} fusion(bf16[1024,512]{1,0:T(8,128)(2,1)} %all-gather.6.cloned.1.call-done, bf16[1024,2048]{1,0:T(8,128)(2,1)} %bitcast.29), kind=kOutput, calls=%fused_computation.3 | convolution fusion | flops 2148532224 | bytes 7340032 | tf_op jit(solution)/shard_map/dot_general | solution.py:96
  321.9 0.2 reduce-scatter.13.cloned.1.call-start
  322.1 0.0 all-gather.8.cloned.1.call-done
  322.2 6.3 %convolution_convert_fusion.4 = bf16[1024,512]{1,0:T(8,128)(2,1)} fusion(bf16[1024,2048]{1,0:T(8,128)(2,1)} %all-gather.8.cloned.1.call-done, bf16[2048,512]{1,0:T(8,128)(2,1)} %param.10), kind=kOutput, calls=%fused_computation.12 | convolution fusion | flops 2148007936 | bytes 7340032 | tf_op jit(solution)/shard_map/dot_general | solution.py:63
  328.5 0.0 reduce-scatter.17.cloned.1.call-start
  328.5 6.2 %convolution_convert_fusion.2 = bf16[2048,512]{1,0:T(8,128)(2,1)} fusion(bf16[1024,2048]{1,0:T(8,128)(2,1)} %all-gather.8.cloned.1.call-done, bf16[1024,512]{1,0:T(8,128)(2,1)} %all-gather.4.cloned.1.call-done), kind=kOutput, calls=%fused_computation.2 | convolution fusion | flops 2148532224 | bytes 7340032 | tf_op jit(solution)/shard_map/dot_general | solution.py:74
  334.8 53.0 %reduce-scatter.11.cloned.1.call-done = bf16[128,512]{1,0:T(8,128)(2,1)} async-done(((bf16[1024,512]{1,0:T(8,128)(2,1)}), bf16[128,512]{1,0:T(8,128)(2,1)}) %reduce-scatter.11.cloned.1.call-update) | async-done | bytes 131088 | tf_op jit(solution)/shard_map/reduce_scatter | solution.py:100
  387.8 1.2 fusion.26
  389.0 12.8 %all-reduce = (f32[128]{0:T(128)S(1)}, f32[128]{0:T(128)S(1)}) all-reduce(f32[128]{0:T(128)S(1)} %get-tuple-element.9, f32[128]{0:T(128)S(1)} %get-tuple-element.10), channel_id=1, replica_groups=mesh['row'=8,'col'=8,'dp'=2] {'row'}, use_global_device_ids=true, to_apply=%region_11.12 | all-reduce | flops 256 | bytes 2048 | tf_op jit(solution)/shard_map/psum | solution.py:117
  401.7 22.4 %reduce-scatter.15.cloned.1.call-done = bf16[512,1024]{1,0:T(8,128)(2,1)} async-done(((bf16[512,2048]{1,0:T(8,128)(2,1)}), bf16[512,1024]{1,0:T(8,128)(2,1)}) %reduce-scatter.15.cloned.1.call-update) | async-done | bytes 1048592 | tf_op jit(solution)/shard_map/reduce_scatter | solution.py:109
  424.1 2.8 convert_element_type.103
  426.9 75.2 %reduce-scatter.13.cloned.1.call-done = bf16[128,512]{1,0:T(8,128)(2,1)} async-done(((bf16[1024,512]{1,0:T(8,128)(2,1)}), bf16[128,512]{1,0:T(8,128)(2,1)}) %reduce-scatter.13.cloned.1.call-update) | async-done | bytes 131088 | tf_op jit(solution)/shard_map/reduce_scatter | solution.py:62
  502.1 1.7 fusion.19
  503.9 0.1 multiply_convert_fusion
  503.9 72.4 %psum.47 = bf16[8,3,512]{2,0,1:T(8,128)(2,1)S(1)} all-reduce(bf16[8,3,512]{2,0,1:T(8,128)(2,1)S(1)} %multiply_convert_fusion), channel_id=1, replica_groups=mesh['row'=8,'col'=8,'dp'=2] {'col','dp'}, use_global_device_ids=true, to_apply=%region_16.17 | all-reduce | flops 12288 | bytes 49152 | tf_op jit(solution)/shard_map/psum | solution.py:128
  576.3 2.3 convolution_bitcast_fusion
  578.6 3.5 copy.10
  582.1 2.8 convert_element_type.105
  (22 shorter events, 0.2 us)
Async XLA Ops:
  7.2 102.8 %copy-start = (bf16[512,2048]{1,0:T(8,128)(2,1)S(1)}, bf16[512,2048]{1,0:T(8,128)(2,1)}, u32[]{:S(2)}) copy-start(bf16[512,2048]{1,0:T(8,128)(2,1)} %param.9) | copy-start | bytes 6291460
  7.2 102.8 %all-gather.6.cloned.1.call-start = ((), (), s32[]{:S(2)}) async-start(), calls=%async_computation.9 | async-start | bytes 1179648 | tf_op jit(solution)/shard_map/all_gather | solution.py:51
  68.0 91.0 %all-gather.4.cloned.1.call-start = ((), (), s32[]{:S(2)}) async-start(), calls=%async_computation.7 | async-start | bytes 1179648 | tf_op jit(solution)/shard_map/all_gather | solution.py:71
  69.7 128.9 %reduce-scatter.9.cloned.1.call-start = ((), (), s32[]{:S(2)}) async-start(), calls=%async_computation.10 | async-start | bytes 4718592 | tf_op jit(solution)/shard_map/reduce_scatter | solution.py:53
  115.5 122.3 %reduce-scatter.7.cloned.1.call-start = ((), (), s32[]{:S(2)}) async-start(), calls=%async_computation.8 | async-start | bytes 4718592 | tf_op jit(solution)/shard_map/reduce_scatter | solution.py:78
  165.3 156.9 %all-gather.8.cloned.1.call-start = ((), (), s32[]{:S(2)}) async-start(), calls=%async_computation.12 | async-start | bytes 4718592 | tf_op jit(solution)/shard_map/all_gather | solution.py:60
  240.6 147.1 %reduce-scatter.11.cloned.1.call-start = ((), (), s32[]{:S(2)}) async-start(), calls=%async_computation.11 | async-start | bytes 1179648 | tf_op jit(solution)/shard_map/reduce_scatter | solution.py:100
  310.3 2.0 copy-start.1
  315.6 108.5 %reduce-scatter.15.cloned.1.call-start = ((), (), s32[]{:S(2)}) async-start(), calls=%async_computation.14 | async-start | bytes 3145728 | tf_op jit(solution)/shard_map/reduce_scatter | solution.py:109
  321.9 180.2 %reduce-scatter.13.cloned.1.call-start = ((), (), s32[]{:S(2)}) async-start(), calls=%async_computation.13 | async-start | bytes 1179648 | tf_op jit(solution)/shard_map/reduce_scatter | solution.py:62
  328.5 59.3 %copy-start.2 = (bf16[128,512]{1,0:T(8,128)(2,1)S(1)}, bf16[128,512]{1,0:T(8,128)(2,1)}, u32[]{:S(2)}) copy-start(bf16[128,512]{1,0:T(8,128)(2,1)} %param.6) | copy-start | bytes 393220
  328.5 253.7 %reduce-scatter.17.cloned.1.call-start = ((), (), s32[]{:S(2)}) async-start(), calls=%async_computation.15 | async-start | bytes 3145728 | tf_op jit(solution)/shard_map/reduce_scatter | solution.py:112
  334.8 167.3 %copy-start.3 = (bf16[128,512]{1,0:T(8,128)(2,1)S(1)}, bf16[128,512]{1,0:T(8,128)(2,1)}, u32[]{:S(2)}) copy-start(bf16[128,512]{1,0:T(8,128)(2,1)} %param.11) | copy-start | bytes 393220
  387.8 114.3 %copy-start.4 = (bf16[128,512]{1,0:T(8,128)(2,1)S(1)}, bf16[128,512]{1,0:T(8,128)(2,1)}, u32[]{:S(2)}) copy-start(bf16[128,512]{1,0:T(8,128)(2,1)} %reduce-scatter.11.cloned.1.call-done) | copy-start | bytes 393220
Sparse Core Ops, SparseCore 0:
  68.1 41.8 all-gather.5
  112.9 46.0 all-gather.3
  161.4 37.1 reduce-scatter.8
  200.9 36.9 reduce-scatter.6
  240.8 64.5 all-gather.7
  315.8 71.9 reduce-scatter.10
  390.7 33.4 reduce-scatter.14
  428.4 73.6 reduce-scatter.12
  504.5 33.8 reduce-scatter.16
